TPU v7x, 256 devices: a whole 4x4x8 slice. The times are simulated.
256 devices in a mesh: dp: 64 (over y, z, core), vocab: 4 (over x).
Axes of the slice: x: 4, y: 4, z: 8, core: 2. Of those that a mesh axis runs over, the one named last changes fastest.
Arguments:
- hidden_rows: bfloat16 [16384, 5120], P('dp'), may hold values from -300 to 300, as said below
- plan_lengths: int32 [64], replicated, may hold values from 1 to 256, 8192 in all
- shard_of_class: int32 [64], replicated, may hold values from 0 to 63, each once
- head_weight: bfloat16 [5120, 3072], P(None, 'vocab'), may hold values from -0.078125 to 0.078125
- teacher_logprobs: bfloat16 [8192, 3072], P('dp', 'vocab'), as said below
Outputs:
- row_grad: bfloat16 [16384, 5120], P('dp')
- row_kl: float32 [8192], P('dp')
Inputs may be any that keep to these rules, and one draw needn't show every extreme that they name: `plan_lengths`: the plan lengths sum to 8192 and the longest is exactly 256. `shard_of_class`: each shard is named once. `hidden_rows`: unused slots hold finite values. `teacher_logprobs`: each row is a log-softmax over the 3072 entries, rounded to bfloat16.
All inputs are finite; a program needn't handle non-finite values.
Results may differ from a plain program's by a relative error of at most 0.0046.
Values may be sent and summed in bfloat16 or wider, within the bound.
No kernel may reach another device: no remote copies, remote signals or barrier semaphores. Data moves between devices by JAX's collectives and lax.ppermute only.
A program may use at most 64 MiB of HBM per device.

v0:
```python
import jax
import jax.numpy as jnp
from jax import lax
from jax.sharding import PartitionSpec as P

loss_scale = 64.0


def divergence(row_block, teacher_block, live_rows, weight):
    logits = jnp.dot(row_block, weight, preferred_element_type=jnp.float32)
    log_teacher = teacher_block.astype(jnp.float32)
    teacher_prob = jnp.exp(log_teacher)
    own_top = jnp.max(logits, axis=1)
    own_mass = jnp.sum(teacher_prob, axis=1)
    own_cross = jnp.sum(teacher_prob * (log_teacher - logits), axis=1)
    row_top = lax.pmax(own_top, "vocab")
    own_total = jnp.sum(jnp.exp(logits - row_top[:, None]), axis=1)
    exp_total, prob_total, cross_term = lax.psum((own_total, own_mass, own_cross), "vocab")
    log_total = row_top + jnp.log(exp_total)
    row_div = (cross_term + prob_total * log_total) * live_rows
    grad_logits = (
        loss_scale
        * (prob_total[:, None] * jnp.exp(logits - log_total[:, None]) - teacher_prob)
        * live_rows[:, None]
    ).astype(jnp.bfloat16)
    partial_grad = lax.dot_general(
        grad_logits, weight, (((1,), (1,)), ((), ())), preferred_element_type=jnp.float32
    )
    hidden_grad = lax.psum(partial_grad, "vocab").astype(jnp.bfloat16)
    return (hidden_grad, row_div)


def body(hidden_rows, plan_lengths, shard_of_class, head_weight, teacher_logprobs):
    shards = lax.axis_size("dp")
    myself = lax.axis_index("dp")
    source_slots = hidden_rows.shape[0]
    feature_width = hidden_rows.shape[1]
    slot_depth = source_slots // shards
    balanced = teacher_logprobs.shape[0]
    offsets = jnp.cumsum(plan_lengths) - plan_lengths
    classes = jnp.arange(shards, dtype=jnp.int32)
    inverse = jnp.sum(
        jnp.where(shard_of_class[None, :] == classes[:, None], classes[None, :], 0), axis=1
    )
    own_offset = offsets[myself]
    column_of = (inverse - own_offset) % shards
    shard_at = shard_of_class[(own_offset + classes) % shards]
    rank_rows = jnp.arange(slot_depth, dtype=jnp.int32)[:, None]
    recv_row = rank_rows * shards + ((inverse[myself] - offsets) % shards)[None, :]
    recv_live = recv_row < plan_lengths[None, :]
    recv_slot = jnp.where(recv_live, (offsets[None, :] + recv_row) // shards, balanced)
    safe_slot = jnp.minimum(recv_slot, balanced - 1).reshape(-1)
    outgoing = jnp.take(hidden_rows.reshape(slot_depth, shards, feature_width), column_of, axis=1)
    arriving = lax.all_to_all(outgoing, "dp", split_axis=1, concat_axis=1, tiled=True)
    flattened = arriving.reshape(slot_depth * shards, feature_width)
    live_rows = recv_live.reshape(-1).astype(jnp.float32)
    teacher_slots = jnp.take(teacher_logprobs, safe_slot, axis=0)
    returning, row_div = divergence(flattened, teacher_slots, live_rows, head_weight)
    row_kl = jnp.zeros((balanced,), jnp.float32).at[recv_slot.reshape(-1)].add(row_div, mode="drop")
    share_width = returning.shape[1]
    returned = lax.all_to_all(
        returning.reshape(slot_depth, shards, share_width),
        "dp",
        split_axis=1,
        concat_axis=1,
        tiled=True,
    )
    grad_share = jnp.take(returned, shard_at, axis=1).reshape(source_slots, share_width)
    return (grad_share, row_kl)


def solution(mesh):
    return jax.shard_map(
        body,
        mesh=mesh,
        in_specs=(P("dp", None), P(), P(), P(None, "vocab"), P("dp", "vocab")),
        out_specs=(P("dp", None), P("dp")),
        check_vma=False,
    )
```

profile of v0, /device:TPU:1, one launch (start us, length us, event | category | flops | bytes accessed | tf_op | source)
XLA Modules:
  0.0 298.8 jit_solution(14799237197427120690)
XLA Ops:
  0.6 0.0 copy-start
  0.6 0.8 select_reduce_fusion
  1.5 0.8 copy.15
  2.2 0.1 reduce-window.9
  2.3 0.1 reduce
  2.4 0.6 dynamic_slice.6
  3.0 1.3 and_select_fusion.4
  4.3 0.6 dynamic_slice.7
  4.9 0.7 compare_and_fusion.1
  5.6 3.8 %copy.16 = bf16[4,64,5120]{2,0,1:T(4,128)(2,1)S(1)} copy(bf16[4,64,5120]{2,1,0:T(8,128)(2,1)} %bitcast.18) | data formatting | bytes 5242880 | tf_op jit(solution)/shard_map/reshape | solution.py:53
  9.3 4.2 %gather_fusion.2 = bf16[64,4,5120]{2,1,0:T(4,128)(2,1)} fusion(bf16[4,64,5120]{2,0,1:T(4,128)(2,1)S(1)} %copy.16, s32[1024]{0:T(1024)S(1)} %pad_clamp_fusion.1), kind=kCustom, calls=%fused_computation.clone | custom fusion | bytes 5243136 | tf_op jit(solution)/shard_map/jit(_take)/gather | solution.py:53
  13.5 4.5 %select_bitcast_fusion.1 = bf16[4,64,5120]{2,0,1:T(4,128)(2,1)} fusion(bf16[64,4,5120]{2,1,0:T(4,128)(2,1)} %gather_fusion.2, pred[64]{0:T(512)(128)(4,1)S(1)} %get-tuple-element.14), kind=kLoop, calls=%fused_computation.6 | loop fusion | flops 1310720 | bytes 5242944 | tf_op jit(solution)/shard_map/jit(_take)/select_n | solution.py:53
  18.0 0.0 copy-start.2
  18.0 13.3 %all-to-all-start = ((bf16[4,64,5120]{2,0,1:T(4,128)(2,1)}), bf16[4,64,5120]{2,0,1:T(4,128)(2,1)S(1)}, u32[]{:S(2)}, u32[]{:S(2)}) async-start(bf16[4,64,5120]{2,0,1:T(4,128)(2,1)} %select_bitcast_fusion.1), calls=%async_computation | async-start | bytes 5242880 | tf_op jit(solution)/shard_map/all_to_all | solution.py:54
  31.3 0.1 add_add_fusion
  31.4 0.1 add.183
  31.5 0.1 add.185
  31.5 0.0 copy-done.2
  31.5 0.1 add_compare_fusion
  31.6 0.1 lt.100
  31.7 0.1 lt.102
  31.8 0.0 copy-done
  31.8 1.2 gather_fusion
  33.1 60.5 %all-to-all-done = bf16[4,64,5120]{2,0,1:T(4,128)(2,1)S(1)} async-done(((bf16[4,64,5120]{2,0,1:T(4,128)(2,1)}), bf16[4,64,5120]{2,0,1:T(4,128)(2,1)S(1)}, u32[]{:S(2)}, u32[]{:S(2)}) %all-to-all-start) | async-done | bytes 2621472 | tf_op jit(solution)/shard_map/all_to_all | solution.py:54
  93.5 0.8 copy.17
  94.3 5.5 %fusion.19 = (f32[256]{0:T(256)S(1)}, f32[256,768]{1,0:T(8,128)S(1)}) fusion(bf16[256,5120]{1,0:T(8,128)(2,1)S(1)} %bitcast.21, bf16[5120,768]{1,0:T(8,128)(2,1)} %param.10), kind=kOutput, calls=%fused_computation.66 | convolution fusion | flops 2013462272 | bytes 11273216 | tf_op jit(solution)/shard_map/dot_general | solution.py:10
  99.9 8.5 %pmax.7 = f32[256]{0:T(256)S(1)} all-reduce(f32[256]{0:T(256)S(1)} %get-tuple-element.16), channel_id=1, replica_groups=mesh['dp'=64,'vocab'=4] {'vocab'}, use_global_device_ids=true, to_apply=%region_5.7 | all-reduce | flops 256 | bytes 2048 | tf_op jit(solution)/shard_map/pmax | solution.py:16
  108.3 0.6 fusion.5
  108.9 6.2 %all-reduce.1 = (f32[256]{0:T(256)S(1)}, f32[256]{0:T(256)S(1)}) all-reduce(f32[256]{0:T(256)S(1)} %get-tuple-element.4, f32[256]{0:T(256)S(1)} %get-tuple-element.5), channel_id=1, replica_groups=mesh['dp'=64,'vocab'=4] {'vocab'}, use_global_device_ids=true, to_apply=%region_7.9 | all-reduce | flops 512 | bytes 4096 | tf_op jit(solution)/shard_map/psum | solution.py:18
  115.1 8.0 %fusion.6 = f32[256,5120]{1,0:T(8,128)} fusion(bf16[5120,768]{1,0:T(8,128)(2,1)} %param.10, f32[256,768]{1,0:T(8,128)S(1)} %get-tuple-element.17, f32[256]{0:T(256)S(1)} %broadcast_select_fusion.1, f32[256]{0:T(256)S(1)} %log_add_fusion, f32[256]{0:T(256)S(1)} %get-tuple-element.9, bf16[256,768]{1,0:T(8,128)(2,1)S(1)} %gather_fusion, ...), kind=kOutput, calls=%fused_computation.16 | convolution fusion | flops 2014642176 | bytes 14290176 | tf_op jit(solution)/shard_map/dot_general | solution.py:26
  123.1 89.4 %all-reduce.3 = (bf16[256,5120]{1,0:T(8,128)(2,1)S(1)}, f32[256]{0:T(256)S(1)}) all-reduce(f32[256,5120]{1,0:T(8,128)} %fusion.6, f32[256]{0:T(256)S(1)} %get-tuple-element.3), channel_id=1, replica_groups=mesh['dp'=64,'vocab'=4] {'vocab'}, use_global_device_ids=true, to_apply=%region_8.10 | all-reduce | flops 1310976 | bytes 7866368 | tf_op jit(solution)/shard_map/psum | solution.py:29
  212.5 3.5 %copy.18 = bf16[4,64,5120]{2,0,1:T(4,128)(2,1)} copy(bf16[4,64,5120]{2,1,0:T(8,128)(2,1)S(1)} %bitcast.20) | data formatting | bytes 5242880 | tf_op jit(solution)/shard_map/reshape | solution.py:62
  216.0 0.0 copy-start.1
  216.0 11.2 %all-to-all-start.1 = ((bf16[4,64,5120]{2,0,1:T(4,128)(2,1)}), bf16[4,64,5120]{2,0,1:T(4,128)(2,1)S(1)}, u32[]{:S(2)}, u32[]{:S(2)}) async-start(bf16[4,64,5120]{2,0,1:T(4,128)(2,1)} %copy.18), calls=%async_computation.1 | async-start | bytes 5242880 | tf_op jit(solution)/shard_map/all_to_all | solution.py:61
  227.1 0.7 fusion.15
  227.8 0.0 copy-done.1
  227.8 0.8 gather_fusion.1
  228.6 2.8 scatter_custom_fusion
  231.5 57.9 %all-to-all-done.1 = bf16[4,64,5120]{2,0,1:T(4,128)(2,1)S(1)} async-done(((bf16[4,64,5120]{2,0,1:T(4,128)(2,1)}), bf16[4,64,5120]{2,0,1:T(4,128)(2,1)S(1)}, u32[]{:S(2)}, u32[]{:S(2)}) %all-to-all-start.1) | async-done | bytes 2621472 | tf_op jit(solution)/shard_map/all_to_all | solution.py:61
  289.4 4.2 %gather_fusion.3 = bf16[64,4,5120]{2,1,0:T(4,128)(2,1)} fusion(bf16[4,64,5120]{2,0,1:T(4,128)(2,1)S(1)} %all-to-all-done.1, s32[1024]{0:T(1024)S(1)} %pad_clamp_fusion), kind=kCustom, calls=%fused_computation.1.clone | custom fusion | bytes 5243136 | tf_op jit(solution)/shard_map/jit(_take)/gather | solution.py:68
  293.5 3.0 %select_bitcast_fusion = bf16[4,64,5120]{2,0,1:T(4,128)(2,1)S(1)} fusion(bf16[64,4,5120]{2,1,0:T(4,128)(2,1)} %gather_fusion.3, pred[64]{0:T(512)(128)(4,1)S(1)} %compare_and_fusion), kind=kLoop, calls=%fused_computation.5 | loop fusion | flops 1310720 | bytes 5242944 | tf_op jit(solution)/shard_map/jit(_take)/select_n | solution.py:68
  296.5 2.3 copy.19
  (13 shorter events, 0.1 us)
Async XLA Ops:
  0.6 31.2 %copy-start = (bf16[128,768]{1,0:T(8,128)(2,1)S(1)}, bf16[128,768]{1,0:T(8,128)(2,1)}, u32[]{:S(2)}) copy-start(bf16[128,768]{1,0:T(8,128)(2,1)} %param.11) | copy-start | bytes 589828
  18.0 13.5 %copy-start.2 = (s32[64]{0:T(128)S(1)}, s32[64]{0:T(128)}, u32[]{:S(2)}) copy-start(s32[64]{0:T(128)} %param.8) | copy-start | bytes 772
  18.0 75.5 %all-to-all-start = ((bf16[4,64,5120]{2,0,1:T(4,128)(2,1)}), bf16[4,64,5120]{2,0,1:T(4,128)(2,1)S(1)}, u32[]{:S(2)}, u32[]{:S(2)}) async-start(bf16[4,64,5120]{2,0,1:T(4,128)(2,1)} %select_bitcast_fusion.1), calls=%async_computation | async-start | bytes 5242880 | tf_op jit(solution)/shard_map/all_to_all | solution.py:54
  216.0 11.8 %copy-start.1 = (s32[64]{0:T(128)S(1)}, s32[64]{0:T(128)}, u32[]{:S(2)}) copy-start(s32[64]{0:T(128)} %param.9) | copy-start | bytes 772
  216.0 73.4 %all-to-all-start.1 = ((bf16[4,64,5120]{2,0,1:T(4,128)(2,1)}), bf16[4,64,5120]{2,0,1:T(4,128)(2,1)S(1)}, u32[]{:S(2)}, u32[]{:S(2)}) async-start(bf16[4,64,5120]{2,0,1:T(4,128)(2,1)} %copy.18), calls=%async_computation.1 | async-start | bytes 5242880 | tf_op jit(solution)/shard_map/all_to_all | solution.py:61
where the time goes:
time: 299 us
  waiting for transfers between devices  118 us (39%)
  blocking collectives  104 us (35%)
  starting transfers between devices  24.4 us (8%)
  local copies, waits for them, and re-layouts  22.9 us (8%)
  other arithmetic  14.8 us (5%)
  matrix products  13.5 us (5%)
    psum x1, blocking collectives, divergence(): hidden_grad = lax.psum(partial_grad, 'vocab').astype(jnp.bfloat16)  89.4 us
    all_to_all x1, waiting for transfers between devices, body(): lax.all_to_all(outgoing, 'dp', split_axis=1, concat_axis=1, tiled=True)  60.5 us
    all_to_all x1, waiting for transfers between devices, body(): lax.all_to_all(returning.reshape(slot_depth, shards, share_width), 'dp',...  57.9 us
    all_to_all x1, starting transfers between devices, body(): lax.all_to_all(outgoing, 'dp', split_axis=1, concat_axis=1, tiled=True)  13.3 us
    all_to_all x1, starting transfers between devices, body(): lax.all_to_all(returning.reshape(slot_depth, shards, share_width), 'dp',...  11.2 us
    pmax x1, blocking collectives, divergence(): row_top = lax.pmax(own_top, 'vocab')  8.47 us
    dot_general x1, matrix products, divergence(): lax.dot_general(grad_logits, weight, (((1,), (1,)), ((), ())), preferred_...  7.99 us
    psum x1, blocking collectives, divergence(): lax.psum((own_total, own_mass, own_cross), 'vocab')  6.18 us
  transfers between devices with their start and end apart: 2, of which 2 were waited for; matrix products, arithmetic and copies ran while one was open for 2% of the time, Pallas kernels for 0%

commit v1 on v0

--- a/solution.py
+++ b/solution.py
@@ -26,7 +26,7 @@
     partial_grad = lax.dot_general(
         grad_logits, weight, (((1,), (1,)), ((), ())), preferred_element_type=jnp.float32
     )
-    hidden_grad = lax.psum(partial_grad, "vocab").astype(jnp.bfloat16)
+    hidden_grad = jnp.sum(lax.all_gather(partial_grad, "vocab"), axis=0).astype(jnp.bfloat16)
     return (hidden_grad, row_div)
 
 

time: 299 us -> 423 us (1.41)
  waiting for transfers between devices: 118 us -> 310 us
  blocking collectives: 104 us -> 14.7 us
  between operations: 0.79 us -> 14.2 us
  other arithmetic: 14.8 us -> 23.8 us
    all_gather x0 -> x1, waiting for transfers between devices: none -> 191 us  [divergence(): lax.all_gather(partial_grad, 'vocab')]
    psum x1 -> x0, blocking collectives: 89.4 us -> none  [divergence(): hidden_grad = lax.psum(partial_grad, 'vocab').astype(jnp.bfloat16)]
    reduce_sum x0 -> x1, other arithmetic: none -> 8.99 us  [divergence(): jnp.sum(lax.all_gather(partial_grad, 'vocab'), axis=0).astype(jnp.bfloat16)]
  transfers between devices with their start and end apart: 2 -> 3, of which waited for: 2 -> 3; matrix products, arithmetic and copies ran while one was open for 2% -> 1% of each run, Pallas kernels for 0% -> 0%
where the time goes in v1:
time: 423 us
  waiting for transfers between devices  310 us (73%)
  starting transfers between devices  24.3 us (6%)
  other arithmetic  23.8 us (6%)
  local copies, waits for them, and re-layouts  22.9 us (5%)
  blocking collectives  14.7 us (3%)
  between operations  14.2 us (3%)
  matrix products  13.5 us (3%)
    all_gather x1, waiting for transfers between devices, divergence(): lax.all_gather(partial_grad, 'vocab')  191 us
    all_to_all x1, waiting for transfers between devices, body(): lax.all_to_all(outgoing, 'dp', split_axis=1, concat_axis=1, tiled=True)  60.4 us
    all_to_all x1, waiting for transfers between devices, body(): lax.all_to_all(returning.reshape(slot_depth, shards, share_width), 'dp',...  57.9 us
    all_to_all x1, starting transfers between devices, body(): lax.all_to_all(outgoing, 'dp', split_axis=1, concat_axis=1, tiled=True)  13.3 us
    all_to_all x1, starting transfers between devices, body(): lax.all_to_all(returning.reshape(slot_depth, shards, share_width), 'dp',...  11 us
    reduce_sum x1, other arithmetic, divergence(): jnp.sum(lax.all_gather(partial_grad, 'vocab'), axis=0).astype(jnp.bfloat16)  8.99 us
    pmax x1, blocking collectives, divergence(): row_top = lax.pmax(own_top, 'vocab')  8.47 us
  transfers between devices with their start and end apart: 3, of which 3 were waited for; matrix products, arithmetic and copies ran while one was open for 1% of the time, Pallas kernels for 0%

profile of v1, /device:TPU:1, one launch (start us, length us, event | category | flops | bytes accessed | tf_op | source)
XLA Modules:
  0.0 422.9 jit_solution(1654084126162623826)
XLA Ops:
  7.2 0.0 copy-start
  7.2 0.8 select_reduce_fusion
  8.0 0.8 copy.14
  8.7 0.1 reduce-window.9
  8.8 0.1 reduce
  8.9 0.6 dynamic_slice.6
  9.5 1.3 and_select_fusion.4
  10.9 0.6 dynamic_slice.7
  11.4 0.7 compare_and_fusion.1
  12.1 3.8 copy.15
  15.9 4.2 gather_fusion.2
  20.0 4.5 %select_bitcast_fusion.1 = bf16[4,64,5120]{2,0,1:T(4,128)(2,1)} fusion(bf16[64,4,5120]{2,1,0:T(4,128)(2,1)} %gather_fusion.2, pred[64]{0:T(512)(128)(4,1)S(1)} %get-tuple-element.15), kind=kLoop, calls=%fused_computation.6 | loop fusion | flops 1310720 | bytes 5242944 | tf_op jit(solution)/shard_map/jit(_take)/select_n | solution.py:53
  24.5 0.0 copy-start.2
  24.5 13.3 %all-to-all-start = ((bf16[4,64,5120]{2,0,1:T(4,128)(2,1)}), bf16[4,64,5120]{2,0,1:T(4,128)(2,1)S(1)}, u32[]{:S(2)}, u32[]{:S(2)}) async-start(bf16[4,64,5120]{2,0,1:T(4,128)(2,1)} %select_bitcast_fusion.1), calls=%async_computation | async-start | bytes 5242880 | tf_op jit(solution)/shard_map/all_to_all | solution.py:54
  37.8 0.0 all-gather.3.cloned.1.call-start
  37.9 0.1 add_add_fusion
  38.0 0.1 add.183
  38.0 0.1 add.181
  38.1 0.0 copy-done.2
  38.1 0.1 add_compare_fusion
  38.2 0.1 lt.102
  38.3 0.1 lt.100
  38.4 0.0 copy-done
  38.4 1.2 gather_fusion
  39.6 60.4 %all-to-all-done = bf16[4,64,5120]{2,0,1:T(4,128)(2,1)S(1)} async-done(((bf16[4,64,5120]{2,0,1:T(4,128)(2,1)}), bf16[4,64,5120]{2,0,1:T(4,128)(2,1)S(1)}, u32[]{:S(2)}, u32[]{:S(2)}) %all-to-all-start) | async-done | bytes 2621472 | tf_op jit(solution)/shard_map/all_to_all | solution.py:54
  100.1 0.8 copy.16
  100.8 5.5 %fusion.19 = (f32[256]{0:T(256)S(1)}, f32[256,768]{1,0:T(8,128)S(1)}) fusion(bf16[256,5120]{1,0:T(8,128)(2,1)S(1)} %bitcast.23, bf16[5120,768]{1,0:T(8,128)(2,1)} %param.10), kind=kOutput, calls=%fused_computation.66 | convolution fusion | flops 2013462272 | bytes 11273216 | tf_op jit(solution)/shard_map/dot_general | solution.py:10
  106.4 8.5 %pmax.7 = f32[256]{0:T(256)S(1)} all-reduce(f32[256]{0:T(256)S(1)} %get-tuple-element.18), channel_id=1, replica_groups=mesh['dp'=64,'vocab'=4] {'vocab'}, use_global_device_ids=true, to_apply=%region_5.7 | all-reduce | flops 256 | bytes 2048 | tf_op jit(solution)/shard_map/pmax | solution.py:16
  114.9 0.6 fusion.5
  115.4 6.2 %all-reduce = (f32[256]{0:T(256)S(1)}, f32[256]{0:T(256)S(1)}, f32[256]{0:T(256)S(1)}) all-reduce(f32[256]{0:T(256)S(1)} %get-tuple-element.4, f32[256]{0:T(256)S(1)} %get-tuple-element.5, f32[256]{0:T(256)S(1)} %get-tuple-element.3), channel_id=1, replica_groups=mesh['dp'=64,'vocab'=4] {'vocab'}, use_global_device_ids=true, to_apply=%region_7.9 | all-reduce | flops 768 | bytes 6144 | tf_op jit(solution)/shard_map/psum | solution.py:18
  121.6 8.0 %fusion.6 = f32[256,5120]{1,0:T(8,128)} fusion(bf16[5120,768]{1,0:T(8,128)(2,1)} %param.10, f32[256,768]{1,0:T(8,128)S(1)} %get-tuple-element.19, f32[256]{0:T(256)S(1)} %get-tuple-element.17, f32[256]{0:T(256)S(1)} %get-tuple-element.10, f32[256]{0:T(256)S(1)} %get-tuple-element.7, bf16[256,768]{1,0:T(8,128)(2,1)S(1)} %gather_fusion, ...), kind=kOutput, calls=%fused_computation.16 | convolution fusion | flops 2014642176 | bytes 14290176 | tf_op jit(solution)/shard_map/dot_general | solution.py:26
  129.6 0.0 all-gather.3.cloned.1.call-update
  129.7 191.2 %all-gather.3.cloned.1.call-done = f32[1024,5120]{1,0:T(8,128)} async-done(((f32[256,5120]{1,0:T(8,128)}), f32[1024,5120]{1,0:T(8,128)}) %all-gather.3.cloned.1.call-update) | async-done | bytes 20971536 | tf_op jit(solution)/shard_map/all_gather | solution.py:29
  320.8 9.0 %reduce_sum.48 = bf16[256,5120]{1,0:T(8,128)(2,1)S(1)} reduce(f32[4,256,5120]{2,1,0:T(8,128)} %bitcast.19, f32[]{:T(128)} %constant.86.clone.1), dimensions={0}, to_apply=%region_8.10 | reduce | flops 3932160 | bytes 23592964 | tf_op jit(solution)/shard_map/reduce_sum | solution.py:29
  329.8 3.5 copy.17
  333.3 0.0 copy-start.1
  333.3 11.0 %all-to-all-start.1 = ((bf16[4,64,5120]{2,0,1:T(4,128)(2,1)}), bf16[4,64,5120]{2,0,1:T(4,128)(2,1)S(1)}, u32[]{:S(2)}, u32[]{:S(2)}) async-start(bf16[4,64,5120]{2,0,1:T(4,128)(2,1)} %copy.17), calls=%async_computation.1 | async-start | bytes 5242880 | tf_op jit(solution)/shard_map/all_to_all | solution.py:61
  344.3 0.7 fusion.15
  345.0 0.0 copy-done.1
  345.0 0.8 gather_fusion.1
  345.8 2.8 scatter_custom_fusion
  348.7 57.9 %all-to-all-done.1 = bf16[4,64,5120]{2,0,1:T(4,128)(2,1)S(1)} async-done(((bf16[4,64,5120]{2,0,1:T(4,128)(2,1)}), bf16[4,64,5120]{2,0,1:T(4,128)(2,1)S(1)}, u32[]{:S(2)}, u32[]{:S(2)}) %all-to-all-start.1) | async-done | bytes 2621472 | tf_op jit(solution)/shard_map/all_to_all | solution.py:61
  406.6 4.2 gather_fusion.3
  410.7 3.0 select_bitcast_fusion
  413.7 2.3 copy.18
  (11 shorter events, 0.1 us)
Async XLA Ops:
  7.2 31.3 %copy-start = (bf16[128,768]{1,0:T(8,128)(2,1)S(1)}, bf16[128,768]{1,0:T(8,128)(2,1)}, u32[]{:S(2)}) copy-start(bf16[128,768]{1,0:T(8,128)(2,1)} %param.11) | copy-start | bytes 589828
  24.5 13.6 %copy-start.2 = (s32[64]{0:T(128)S(1)}, s32[64]{0:T(128)}, u32[]{:S(2)}) copy-start(s32[64]{0:T(128)} %param.8) | copy-start | bytes 772
  24.5 75.5 %all-to-all-start = ((bf16[4,64,5120]{2,0,1:T(4,128)(2,1)}), bf16[4,64,5120]{2,0,1:T(4,128)(2,1)S(1)}, u32[]{:S(2)}, u32[]{:S(2)}) async-start(bf16[4,64,5120]{2,0,1:T(4,128)(2,1)} %select_bitcast_fusion.1), calls=%async_computation | async-start | bytes 5242880 | tf_op jit(solution)/shard_map/all_to_all | solution.py:54
  37.8 283.0 %all-gather.3.cloned.1.call-start = ((), (), s32[]{:S(2)}) async-start(), calls=%async_computation.2 | async-start | bytes 26214400 | tf_op jit(solution)/shard_map/all_gather | solution.py:29
  333.3 11.7 %copy-start.1 = (s32[64]{0:T(128)S(1)}, s32[64]{0:T(128)}, u32[]{:S(2)}) copy-start(s32[64]{0:T(128)} %param.9) | copy-start | bytes 772
  333.3 73.2 %all-to-all-start.1 = ((bf16[4,64,5120]{2,0,1:T(4,128)(2,1)}), bf16[4,64,5120]{2,0,1:T(4,128)(2,1)S(1)}, u32[]{:S(2)}, u32[]{:S(2)}) async-start(bf16[4,64,5120]{2,0,1:T(4,128)(2,1)} %copy.17), calls=%async_computation.1 | async-start | bytes 5242880 | tf_op jit(solution)/shard_map/all_to_all | solution.py:61
Sparse Core Ops, SparseCore 0:
  129.8 190.9 all-gather.2
